TPU v7x, 256 devices: a whole 4x4x8 slice. The times are simulated.
256 devices in a mesh: section: 4 (over x), seq: 16 (over z, y_hi), tp: 4 (over y_lo, core).
Axes of the slice: x: 4, y: 4 (y_hi: 2, y_lo: 2; y = y_hi * 2 + y_lo), z: 8, core: 2. Of those that a mesh axis runs over, the one named last changes fastest.
Arguments:
- queries: bfloat16 [4, 4096, 8192], P('section', 'seq', 'tp'), may hold values from -135 to 135
- upstream: bfloat16 [4, 4096, 8192], P('section', 'seq', 'tp'), may hold values from -48 to 48
- shared_kv: bfloat16 [2, 4096, 1024], P(None, ('seq', 'tp')), may hold values from -5 to 5
Outputs:
- d_queries: bfloat16 [4, 4096, 8192], P('section', 'seq', 'tp')
- d_shared_kv: float32 [2, 4096, 1024], P(None, ('seq', 'tp'))
All inputs are finite; a program needn't handle non-finite values.
Results may differ from a plain program's by a relative error of at most 0.0098.
Values may be sent and summed in bfloat16 or wider, within the bound.
No kernel may reach another device: no remote copies, remote signals or barrier semaphores. Data moves between devices by JAX's collectives and lax.ppermute only.
A program may use at most 128 MiB of HBM per device.

v0:
```python
import math
import jax
import jax.numpy as jnp
from jax import lax
from jax.sharding import PartitionSpec as P

QH = 64
KVH = 8
HD = 128
WINDOW = 1024


def shifted(value, axis, by):
    peers = lax.axis_size(axis)
    pairs = [(i, i + by) for i in range(peers) if 0 <= i + by < peers]
    return lax.ppermute(value, axis, pairs)


def head_grads(query_block, grad_block, keys_head, values_head, allowed, score_scale):
    scores = (
        jnp.einsum("rgd,ed->gre", query_block, keys_head, preferred_element_type=jnp.float32)
        * score_scale
    )
    masked = jnp.where(allowed[None], scores, -jnp.inf)
    highest = jnp.max(masked, axis=-1, keepdims=True)
    weights = jnp.exp(masked - highest)
    probs = weights / jnp.sum(weights, axis=-1, keepdims=True)
    probs_b = probs.astype(jnp.bfloat16)
    attn_out = jnp.einsum("gre,ed->rgd", probs_b, values_head, preferred_element_type=jnp.float32)
    delta = jnp.sum(grad_block.astype(jnp.float32) * attn_out, axis=-1)
    dprobs = jnp.einsum("rgd,ed->gre", grad_block, values_head, preferred_element_type=jnp.float32)
    dscores = probs * (dprobs - jnp.transpose(delta)[:, :, None])
    dscores_b = dscores.astype(jnp.bfloat16)
    grad_query = (
        jnp.einsum("gre,ed->rgd", dscores_b, keys_head, preferred_element_type=jnp.float32)
        * score_scale
    )
    grad_key = (
        jnp.einsum("gre,rgd->ed", dscores_b, query_block, preferred_element_type=jnp.float32)
        * score_scale
    )
    grad_value = jnp.einsum("gre,rgd->ed", probs_b, grad_block, preferred_element_type=jnp.float32)
    return (grad_query, grad_key, grad_value)


def body(queries, upstream, shared_kv):
    local_kv = lax.all_to_all(shared_kv, "tp", split_axis=2, concat_axis=1, tiled=True)
    tok_rows = local_kv.shape[1]
    kv_cols = local_kv.shape[2]
    head_size = HD
    local_kv_heads = kv_cols // head_size
    group_size = QH // KVH
    block_heads = max(1, group_size // 2)
    span_blocks = WINDOW // tok_rows
    score_scale = 1.0 / math.sqrt(head_size)
    earlier = [shifted(local_kv, "seq", span_blocks - offset) for offset in range(span_blocks)]
    extended = jnp.concatenate(earlier + [local_kv], axis=1)
    ext_rows = extended.shape[1]
    position = lax.axis_index("seq")
    row_ids = lax.broadcasted_iota(jnp.int32, (tok_rows, ext_rows), 0)
    key_ids = lax.broadcasted_iota(jnp.int32, (tok_rows, ext_rows), 1)
    allowed = (
        (key_ids >= row_ids + 1)
        & (key_ids <= row_ids + WINDOW)
        & (position * tok_rows - WINDOW + key_ids >= 0)
    )
    query_heads = queries.reshape(tok_rows, -1, head_size)
    grad_heads = upstream.reshape(tok_rows, -1, head_size)
    query_parts = []
    key_parts = []
    value_parts = []
    for kv_head in range(local_kv_heads):
        keys_head = extended[0, :, kv_head * head_size : (kv_head + 1) * head_size]
        values_head = extended[1, :, kv_head * head_size : (kv_head + 1) * head_size]
        key_total = jnp.zeros((ext_rows, head_size), jnp.float32)
        value_total = jnp.zeros((ext_rows, head_size), jnp.float32)
        for first_head in range(kv_head * group_size, (kv_head + 1) * group_size, block_heads):
            query_block = query_heads[:, first_head : first_head + block_heads]
            grad_block = grad_heads[:, first_head : first_head + block_heads]
            grad_query, grad_key, grad_value = head_grads(
                query_block, grad_block, keys_head, values_head, allowed, score_scale
            )
            query_parts.append(grad_query)
            key_total = key_total + grad_key
            value_total = value_total + grad_value
        key_parts.append(key_total)
        value_parts.append(value_total)
    d_queries = jnp.concatenate(query_parts, axis=1).reshape(1, tok_rows, -1).astype(jnp.bfloat16)
    grad_ext = jnp.stack([jnp.concatenate(key_parts, axis=1), jnp.concatenate(value_parts, axis=1)])
    own_rows = grad_ext[:, span_blocks * tok_rows :, :]
    for offset in range(span_blocks):
        own_rows = own_rows + shifted(
            grad_ext[:, offset * tok_rows : (offset + 1) * tok_rows, :].astype(jnp.bfloat16),
            "seq",
            offset - span_blocks,
        ).astype(jnp.float32)
    summed = lax.psum(own_rows, "section")
    d_shared_kv = lax.all_to_all(summed, "tp", split_axis=1, concat_axis=2, tiled=True)
    return (d_queries, d_shared_kv)


def solution(mesh):
    in_specs = (P("section", "seq", "tp"), P("section", "seq", "tp"), P(None, ("seq", "tp"), None))
    out_specs = (P("section", "seq", "tp"), P(None, ("seq", "tp"), None))
    return jax.shard_map(body, mesh=mesh, in_specs=in_specs, out_specs=out_specs, check_vma=False)
```

profile of v0, /device:TPU:1, one launch (start us, length us, event | category | flops | bytes accessed | tf_op | source)
XLA Modules:
  0.0 228.5 jit_solution(4104117547018688944)
XLA Ops:
  7.2 1.4 copy.143
  9.6 6.6 %all-to-all-start = ((bf16[4,2,16384]{2,1,0:T(2,128)(2,1)}), bf16[4,2,16384]{2,1,0:T(2,128)(2,1)S(1)}, u32[]{:S(2)}, u32[]{:S(2)}) async-start(bf16[4,2,16384]{2,1,0:T(2,128)(2,1)} %reshape.105), calls=%async_computation | async-start | bytes 524288 | tf_op jit(solution)/shard_map/all_to_all | solution.py:47
  16.2 5.0 %all-to-all-done = bf16[4,2,16384]{2,1,0:T(2,128)(2,1)S(1)} async-done(((bf16[4,2,16384]{2,1,0:T(2,128)(2,1)}), bf16[4,2,16384]{2,1,0:T(2,128)(2,1)S(1)}, u32[]{:S(2)}, u32[]{:S(2)}) %all-to-all-start) | async-done | bytes 262176 | tf_op jit(solution)/shard_map/all_to_all | solution.py:47
  22.6 3.9 %collective-permute-start = (bf16[2,256,256]{2,1,0:T(8,128)(2,1)}, bf16[2,256,256]{2,1,0:T(8,128)(2,1)}, u32[]{:S(2)}, u32[]{:S(2)}) collective-permute-start(bf16[2,256,256]{2,1,0:T(8,128)(2,1)} %bitcast.2), channel_id=1, source_target_pairs={{0,16},{4,20},{8,24},{12,28},{16,32},{20,36},{24,40},{28,44},{32,4... | collective-permute-start | bytes 786440 | tf_op jit(solution)/shard_map/ppermute | solution.py:16
  28.2 4.3 %collective-permute-start.2 = (bf16[2,256,256]{2,1,0:T(8,128)(2,1)}, bf16[2,256,256]{2,1,0:T(8,128)(2,1)}, u32[]{:S(2)}, u32[]{:S(2)}) collective-permute-start(bf16[2,256,256]{2,1,0:T(8,128)(2,1)} %bitcast.2), channel_id=1, source_target_pairs={{0,8},{4,12},{8,16},{12,20},{16,24},{20,28},{24,32},{28,36},{32,40... | collective-permute-start | bytes 786440 | tf_op jit(solution)/shard_map/ppermute | solution.py:16
  32.4 6.7 %collective-permute-start.1 = (bf16[2,256,256]{2,1,0:T(8,128)(2,1)}, bf16[2,256,256]{2,1,0:T(8,128)(2,1)}, u32[]{:S(2)}, u32[]{:S(2)}) collective-permute-start(bf16[2,256,256]{2,1,0:T(8,128)(2,1)} %bitcast.2), channel_id=1, source_target_pairs={{0,12},{4,16},{8,20},{12,24},{16,28},{20,32},{24,36},{28,40},{32,4... | collective-permute-start | bytes 786440 | tf_op jit(solution)/shard_map/ppermute | solution.py:16
  39.2 1.5 copy.145
  44.3 2.6 %collective-permute-start.3 = (bf16[2,256,256]{2,1,0:T(8,128)(2,1)}, bf16[2,256,256]{2,1,0:T(8,128)(2,1)S(1)}, u32[]{:S(2)}, u32[]{:S(2)}) collective-permute-start(bf16[2,256,256]{2,1,0:T(8,128)(2,1)} %bitcast.2), channel_id=1, source_target_pairs={{0,4},{4,8},{8,12},{12,16},{16,20},{20,24},{24,28},{28,32},{32,36}... | collective-permute-start | bytes 786440 | tf_op jit(solution)/shard_map/ppermute | solution.py:16
  51.9 5.3 %exponential_reduce_fusion.3 = (f32[4,256]{1,0:T(4,128)S(1)}, f32[4,256,1280]{1,2,0:T(8,128)}) fusion(pred[256,1280]{0,1:T(8,128)(4,1)} %fusion.28, bf16[256,16,128]{0,2,1:T(8,128)(2,1)S(1)} %bitcast.227, bf16[2,1280,256]{2,1,0:T(8,128)(2,1)S(1)} %constant_dynamic-update-slice_fusion), kind=kOutput, calls=%fused_computation.31 | convolution fusion | flops 340788480 | bytes 6164480 | tf_op jit(solution)/shard_map/sub | solution.py:26
  57.1 5.1 %exponential_reduce_fusion.1 = (f32[4,256]{1,0:T(4,128)S(1)}, f32[4,256,1280]{1,2,0:T(8,128)}) fusion(pred[256,1280]{0,1:T(8,128)(4,1)} %fusion.28, bf16[256,16,128]{0,2,1:T(8,128)(2,1)S(1)} %bitcast.228, bf16[2,1280,256]{2,1,0:T(8,128)(2,1)S(1)} %constant_dynamic-update-slice_fusion), kind=kOutput, calls=%fused_computation.27 | convolution fusion | flops 340788480 | bytes 6164480 | tf_op jit(solution)/shard_map/sub | solution.py:26
  62.3 5.1 %exponential_reduce_fusion.2 = (f32[4,256]{1,0:T(4,128)S(1)}, f32[4,256,1280]{1,2,0:T(8,128)}) fusion(pred[256,1280]{0,1:T(8,128)(4,1)} %fusion.28, bf16[256,16,128]{0,2,1:T(8,128)(2,1)S(1)} %bitcast.229, bf16[2,1280,256]{2,1,0:T(8,128)(2,1)S(1)} %constant_dynamic-update-slice_fusion), kind=kOutput, calls=%fused_computation.29 | convolution fusion | flops 340788480 | bytes 6164480 | tf_op jit(solution)/shard_map/sub | solution.py:26
  67.4 5.1 %exponential_reduce_fusion = (f32[4,256]{1,0:T(4,128)S(1)}, f32[4,256,1280]{1,2,0:T(8,128)}) fusion(pred[256,1280]{0,1:T(8,128)(4,1)} %fusion.28, bf16[256,16,128]{0,2,1:T(8,128)(2,1)S(1)} %bitcast.230, bf16[2,1280,256]{2,1,0:T(8,128)(2,1)S(1)} %constant_dynamic-update-slice_fusion), kind=kOutput, calls=%fused_computation.25 | convolution fusion | flops 340788480 | bytes 6164480 | tf_op jit(solution)/shard_map/sub | solution.py:26
  72.5 4.0 %fusion.23 = bf16[4,256,1280]{1,2,0:T(8,128)(2,1)S(1)} fusion(f32[4,256]{1,0:T(4,128)S(1)} %get-tuple-element.24, f32[4,256,1280]{1,2,0:T(8,128)} %get-tuple-element.25), kind=kLoop, calls=%fused_computation.50 | loop fusion | flops 2621440 | bytes 7868416 | tf_op jit(solution)/shard_map/convert_element_type | solution.py:28
  81.2 1.6 fusion.25
  88.6 1.4 fusion.24
  90.0 1.3 fusion.38
  95.7 1.4 fusion.26
  99.8 2.5 %fusion.9 = bf16[4,256,1280]{1,2,0:T(8,128)(2,1)S(1)} fusion(f32[4,256]{1,0:T(4,128)S(1)} %bitcast.240, f32[4,256]{1,0:T(4,128)S(1)} %get-tuple-element.18, f32[4,256,1280]{1,2,0:T(8,128)S(1)} %bitcast.220, bf16[2,1280,256]{2,1,0:T(8,128)(2,1)S(1)} %copy-done.5, bf16[256,16,128]{0,2,1:T(8,128)(2,1)} %bitcast.218), kind=kOutput, calls=%fused_computation.10 | convolution fusion | flops 340787200 | bytes 8462336 | tf_op jit(solution)/shard_map/rgd,ed->gre/dot_general | solution.py:31
  104.7 1.3 collective-permute-start.4
  106.0 1.3 collective-permute-start.7
  107.3 1.3 collective-permute-start.6
  108.6 1.3 collective-permute-start.5
  110.5 22.5 %collective-permute-done.4 = bf16[2,256,256]{1,2,0:T(8,128)(2,1)S(1)} collective-permute-done((bf16[2,256,256]{1,2,0:T(8,128)(2,1)S(1)}, bf16[2,256,256]{1,2,0:T(8,128)(2,1)S(1)}, u32[]{:S(2)}, u32[]{:S(2)}) %collective-permute-start.4) | collective-permute-done | bytes 262176 | tf_op jit(solution)/shard_map/ppermute | solution.py:16
  133.0 6.1 %collective-permute-done.5 = bf16[2,256,256]{1,2,0:T(8,128)(2,1)S(1)} collective-permute-done((bf16[2,256,256]{1,2,0:T(8,128)(2,1)S(1)}, bf16[2,256,256]{1,2,0:T(8,128)(2,1)S(1)}, u32[]{:S(2)}, u32[]{:S(2)}) %collective-permute-start.5) | collective-permute-done | bytes 262176 | tf_op jit(solution)/shard_map/ppermute | solution.py:16
  140.1 3.2 %fusion.42 = bf16[256,4,128]{0,2,1:T(8,128)(2,1)} fusion(bf16[4,256,1280]{1,2,0:T(8,128)(2,1)} %copy-done.2, bf16[2,1280,256]{2,1,0:T(8,128)(2,1)} %copy-done.4), kind=kOutput, calls=%fused_computation.81 | convolution fusion | flops 335806464 | bytes 3211264 | tf_op jit(solution)/shard_map/gre,ed->rgd/dot_general | solution.py:35
  143.3 2.2 fusion.43
  145.5 59.1 %all-reduce.2.cloned.1.call-done = f32[2,256,256]{1,2,0:T(8,128)} async-done(((f32[2,256,256]{1,2,0:T(8,128)}), f32[2,256,256]{1,2,0:T(8,128)}) %all-reduce.2.cloned.1.call-update) | async-done | bytes 524304 | tf_op jit(solution)/shard_map/psum | solution.py:97
  204.6 2.0 copy.191
  206.6 6.3 %all-to-all-start.1 = ((f32[2,256,256]{2,0,1:T(2,128)}), f32[2,256,256]{2,0,1:T(2,128)S(1)}, u32[]{:S(2)}, u32[]{:S(2)}) async-start(f32[2,256,256]{2,0,1:T(2,128)} %copy.191), calls=%async_computation.1 | async-start | bytes 1048576 | tf_op jit(solution)/shard_map/all_to_all | solution.py:98
  213.0 1.6 fusion.41
  214.7 1.4 copy.194
  216.1 4.7 %all-to-all-done.1 = f32[2,256,256]{2,0,1:T(2,128)S(1)} async-done(((f32[2,256,256]{2,0,1:T(2,128)}), f32[2,256,256]{2,0,1:T(2,128)S(1)}, u32[]{:S(2)}, u32[]{:S(2)}) %all-to-all-start.1) | async-done | bytes 524320 | tf_op jit(solution)/shard_map/all_to_all | solution.py:98
  (98 shorter events, 35.0 us)
Async XLA Ops:
  7.2 20.5 %copy-start.12 = (bf16[1,256,2048]{2,1,0:T(8,128)(2,1)S(1)}, bf16[1,256,2048]{2,1,0:T(8,128)(2,1)}, u32[]{:S(2)}) copy-start(bf16[1,256,2048]{2,1,0:T(8,128)(2,1)} %param.4) | copy-start | bytes 3145732
  9.6 11.6 %all-to-all-start = ((bf16[4,2,16384]{2,1,0:T(2,128)(2,1)}), bf16[4,2,16384]{2,1,0:T(2,128)(2,1)S(1)}, u32[]{:S(2)}, u32[]{:S(2)}) async-start(bf16[4,2,16384]{2,1,0:T(2,128)(2,1)} %reshape.105), calls=%async_computation | async-start | bytes 524288 | tf_op jit(solution)/shard_map/all_to_all | solution.py:47
  16.2 188.4 %all-reduce.2.cloned.1.call-start = ((), (), s32[]{:S(2)}) async-start(), calls=%async_computation.2 | async-start | bytes 1048576 | tf_op jit(solution)/shard_map/psum | solution.py:97
  22.6 24.3 %collective-permute-start = (bf16[2,256,256]{2,1,0:T(8,128)(2,1)}, bf16[2,256,256]{2,1,0:T(8,128)(2,1)}, u32[]{:S(2)}, u32[]{:S(2)}) collective-permute-start(bf16[2,256,256]{2,1,0:T(8,128)(2,1)} %bitcast.2), channel_id=1, source_target_pairs={{0,16},{4,20},{8,24},{12,28},{16,32},{20,36},{24,40},{28,44},{32,4... | collective-permute-start | bytes 786440 | tf_op jit(solution)/shard_map/ppermute | solution.py:16
  28.2 70.3 %copy-start.3 = (bf16[1,256,2048]{1,2,0:T(8,128)(2,1)}, bf16[1,256,2048]{1,2,0:T(8,128)(2,1)S(1)}, u32[]{:S(2)}) copy-start(bf16[1,256,2048]{1,2,0:T(8,128)(2,1)S(1)} %copy.147) | copy-start | bytes 3145732
  28.2 20.7 %collective-permute-start.2 = (bf16[2,256,256]{2,1,0:T(8,128)(2,1)}, bf16[2,256,256]{2,1,0:T(8,128)(2,1)}, u32[]{:S(2)}, u32[]{:S(2)}) collective-permute-start(bf16[2,256,256]{2,1,0:T(8,128)(2,1)} %bitcast.2), channel_id=1, source_target_pairs={{0,8},{4,12},{8,16},{12,20},{16,24},{20,28},{24,32},{28,36},{32,40... | collective-permute-start | bytes 786440 | tf_op jit(solution)/shard_map/ppermute | solution.py:16
  32.4 15.5 %collective-permute-start.1 = (bf16[2,256,256]{2,1,0:T(8,128)(2,1)}, bf16[2,256,256]{2,1,0:T(8,128)(2,1)}, u32[]{:S(2)}, u32[]{:S(2)}) collective-permute-start(bf16[2,256,256]{2,1,0:T(8,128)(2,1)} %bitcast.2), channel_id=1, source_target_pairs={{0,12},{4,16},{8,20},{12,24},{16,28},{20,32},{24,36},{28,40},{32,4... | collective-permute-start | bytes 786440 | tf_op jit(solution)/shard_map/ppermute | solution.py:16
  40.7 45.6 %copy-start.6 = (bf16[1,256,2048]{1,2,0:T(8,128)(2,1)}, bf16[1,256,2048]{1,2,0:T(8,128)(2,1)S(1)}, u32[]{:S(2)}) copy-start(bf16[1,256,2048]{1,2,0:T(8,128)(2,1)S(1)} %copy.145) | copy-start | bytes 3145732
  44.3 6.6 %collective-permute-start.3 = (bf16[2,256,256]{2,1,0:T(8,128)(2,1)}, bf16[2,256,256]{2,1,0:T(8,128)(2,1)S(1)}, u32[]{:S(2)}, u32[]{:S(2)}) collective-permute-start(bf16[2,256,256]{2,1,0:T(8,128)(2,1)} %bitcast.2), channel_id=1, source_target_pairs={{0,4},{4,8},{8,12},{12,16},{16,20},{20,24},{24,28},{28,32},{32,36}... | collective-permute-start | bytes 786440 | tf_op jit(solution)/shard_map/ppermute | solution.py:16
  51.9 45.3 %copy-start.4 = (bf16[2,1280,256]{2,1,0:T(8,128)(2,1)}, bf16[2,1280,256]{2,1,0:T(8,128)(2,1)S(1)}, u32[]{:S(2)}) copy-start(bf16[2,1280,256]{2,1,0:T(8,128)(2,1)S(1)} %constant_dynamic-update-slice_fusion) | copy-start | bytes 3932164
  72.5 6.3 %slice-start.6 = ((s8[5242880]{0:T(1024)(128)(4,1)}), s8[4194304]{0:T(1024)(128)(4,1)S(1)}, s32[]{:S(2)}) async-start(s8[5242880]{0:T(1024)(128)(4,1)} %bitcast.225), calls=%async_computation.9 | async-start | bytes 8388608
  76.5 2.3 %slice-start.7 = ((s8[5242880]{0:T(1024)(128)(4,1)}), s8[1048576]{0:T(1024)(128)(4,1)S(1)}, s32[]{:S(2)}) async-start(s8[5242880]{0:T(1024)(128)(4,1)} %bitcast.225), calls=%async_computation.10 | async-start | bytes 2097152
  78.8 2.2 slice-start.4
  78.8 2.5 %slice-start.5 = ((s8[5242880]{0:T(1024)(128)(4,1)}), s8[1048576]{0:T(1024)(128)(4,1)S(1)}, s32[]{:S(2)}) async-start(s8[5242880]{0:T(1024)(128)(4,1)} %bitcast.223), calls=%async_computation.8 | async-start | bytes 2097152
  85.2 2.7 %slice-start.2 = ((s8[5242880]{0:T(1024)(128)(4,1)}), s8[4194304]{0:T(1024)(128)(4,1)S(1)}, s32[]{:S(2)}) async-start(s8[5242880]{0:T(1024)(128)(4,1)} %bitcast.221), calls=%async_computation.5 | async-start | bytes 8388608
  85.2 3.4 %slice-start.3 = ((s8[5242880]{0:T(1024)(128)(4,1)}), s8[1048576]{0:T(1024)(128)(4,1)S(1)}, s32[]{:S(2)}) async-start(s8[5242880]{0:T(1024)(128)(4,1)} %bitcast.221), calls=%async_computation.6 | async-start | bytes 2097152
  86.3 1.6 copy-start.2
  88.6 1.4 copy-start.9
  92.3 2.4 %slice-start = ((s8[5242880]{0:T(1024)(128)(4,1)}), s8[4194304]{0:T(1024)(128)(4,1)S(1)}, s32[]{:S(2)}) async-start(s8[5242880]{0:T(1024)(128)(4,1)} %bitcast.219), calls=%async_computation.3 | async-start | bytes 8388608
  92.3 3.4 %slice-start.1 = ((s8[5242880]{0:T(1024)(128)(4,1)}), s8[1048576]{0:T(1024)(128)(4,1)S(1)}, s32[]{:S(2)}) async-start(s8[5242880]{0:T(1024)(128)(4,1)} %bitcast.219), calls=%async_computation.4 | async-start | bytes 2097152
  93.5 8.8 %copy-start = (bf16[4,256,1280]{1,2,0:T(8,128)(2,1)}, bf16[4,256,1280]{1,2,0:T(8,128)(2,1)S(1)}, u32[]{:S(2)}) copy-start(bf16[4,256,1280]{1,2,0:T(8,128)(2,1)S(1)} %fusion.13) | copy-start | bytes 7864324
  95.7 1.4 copy-start.8
  98.5 1.3 copy-start.5
  99.8 2.5 %copy-start.7 = (bf16[1,256,2048]{1,2,0:T(8,128)(2,1)S(1)}, bf16[1,256,2048]{1,2,0:T(8,128)(2,1)}, u32[]{:S(2)}) copy-start(bf16[1,256,2048]{1,2,0:T(8,128)(2,1)} %copy-done.6) | copy-start | bytes 3145732
  104.7 28.2 %collective-permute-start.4 = (bf16[2,256,256]{1,2,0:T(8,128)(2,1)S(1)}, bf16[2,256,256]{1,2,0:T(8,128)(2,1)S(1)}, u32[]{:S(2)}, u32[]{:S(2)}) collective-permute-start(bf16[2,256,256]{1,2,0:T(8,128)(2,1)S(1)} %get-tuple-element.10), channel_id=1, source_target_pairs={{16,0},{20,4},{24,8},{28,12},{32,16},{36,20},{40,24},{44,28},{48,3... | collective-permute-start | bytes 786440 | tf_op jit(solution)/shard_map/ppermute | solution.py:16
  106.0 26.9 %collective-permute-start.7 = (bf16[2,256,256]{1,2,0:T(8,128)(2,1)S(1)}, bf16[2,256,256]{1,2,0:T(8,128)(2,1)S(1)}, u32[]{:S(2)}, u32[]{:S(2)}) collective-permute-start(bf16[2,256,256]{1,2,0:T(8,128)(2,1)S(1)} %get-tuple-element.11), channel_id=1, source_target_pairs={{4,0},{8,4},{12,8},{16,12},{20,16},{24,20},{28,24},{32,28},{36,32}... | collective-permute-start | bytes 786440 | tf_op jit(solution)/shard_map/ppermute | solution.py:16
  107.3 25.6 %collective-permute-start.6 = (bf16[2,256,256]{1,2,0:T(8,128)(2,1)S(1)}, bf16[2,256,256]{1,2,0:T(8,128)(2,1)S(1)}, u32[]{:S(2)}, u32[]{:S(2)}) collective-permute-start(bf16[2,256,256]{1,2,0:T(8,128)(2,1)S(1)} %get-tuple-element.12), channel_id=1, source_target_pairs={{8,0},{12,4},{16,8},{20,12},{24,16},{28,20},{32,24},{36,28},{40,32... | collective-permute-start | bytes 786440 | tf_op jit(solution)/shard_map/ppermute | solution.py:16
  108.6 30.4 %collective-permute-start.5 = (bf16[2,256,256]{1,2,0:T(8,128)(2,1)S(1)}, bf16[2,256,256]{1,2,0:T(8,128)(2,1)S(1)}, u32[]{:S(2)}, u32[]{:S(2)}) collective-permute-start(bf16[2,256,256]{1,2,0:T(8,128)(2,1)S(1)} %get-tuple-element.13), channel_id=1, source_target_pairs={{12,0},{16,4},{20,8},{24,12},{28,16},{32,20},{36,24},{40,28},{44,3... | collective-permute-start | bytes 786440 | tf_op jit(solution)/shard_map/ppermute | solution.py:16
  140.1 3.3 %copy-start.1 = (bf16[4,256,1280]{1,2,0:T(8,128)(2,1)S(1)}, bf16[4,256,1280]{1,2,0:T(8,128)(2,1)}, u32[]{:S(2)}) copy-start(bf16[4,256,1280]{1,2,0:T(8,128)(2,1)} %copy-done) | copy-start | bytes 7864324
  206.6 14.2 %all-to-all-start.1 = ((f32[2,256,256]{2,0,1:T(2,128)}), f32[2,256,256]{2,0,1:T(2,128)S(1)}, u32[]{:S(2)}, u32[]{:S(2)}) async-start(f32[2,256,256]{2,0,1:T(2,128)} %copy.191), calls=%async_computation.1 | async-start | bytes 1048576 | tf_op jit(solution)/shard_map/all_to_all | solution.py:98
  213.0 1.6 copy-start.13
  213.0 1.6 copy-start.14
  (2 other events, 2.0 us)
Sparse Core Ops, SparseCore 0:
  140.2 64.3 all-reduce.1
where the time goes:
time: 229 us
  waiting for transfers between devices  98.4 us (43%)
  matrix products  47 us (21%)
  starting transfers between devices  35.5 us (16%)
  local copies, waits for them, and re-layouts  22.1 us (10%)
  between operations  14.6 us (6%)
  other arithmetic  11 us (5%)
    psum x1, waiting for transfers between devices, body(): summed = lax.psum(own_rows, 'section')  59.1 us
    ppermute x8, waiting for transfers between devices, shifted(): return lax.ppermute(value, axis, pairs)  29.6 us
    ppermute x8, starting transfers between devices, shifted(): return lax.ppermute(value, axis, pairs)  22.6 us
    sub x4, matrix products, head_grads(): weights = jnp.exp(masked - highest)  20.6 us
    unnamed x61, local copies, waits for them, and re-layouts  17.1 us
    convert_element_type x4, other arithmetic, head_grads(): probs_b = probs.astype(jnp.bfloat16)  8.43 us
    dot_general x4, matrix products, head_grads(): jnp.einsum('gre,ed->rgd', dscores_b, keys_head, preferred_element_type=jn...  7.58 us
    all_to_all x1, starting transfers between devices, body(): lax.all_to_all(shared_kv, 'tp', split_axis=2, concat_axis=1, tiled=True)  6.57 us
  transfers between devices with their start and end apart: 11, of which 6 were waited for; matrix products, arithmetic and copies ran while one was open for 8% of the time, Pallas kernels for 0%

commit v1 on v0

--- a/solution.py
+++ b/solution.py
@@ -3,6 +3,7 @@
 import jax.numpy as jnp
 from jax import lax
 from jax.sharding import PartitionSpec as P
+from jax.lax import ppermute, psum
 
 QH = 64
 KVH = 8
@@ -94,7 +95,12 @@
             "seq",
             offset - span_blocks,
         ).astype(jnp.float32)
-    summed = lax.psum(own_rows, "section")
+    chips = psum(1, "section")
+    summed = own_rows
+    for nth in [c for c in (1, 2, 4, 8, 16) if c < chips]:
+        frame_out = tuple(((at, at ^ nth) for at in range(chips)))
+        w1 = ppermute(summed, "section", frame_out)
+        summed = summed + w1
     d_shared_kv = lax.all_to_all(summed, "tp", split_axis=1, concat_axis=2, tiled=True)
     return (d_queries, d_shared_kv)
 

time: 229 us -> 191 us (0.83)
  the two profiles are of different devices: /device:TPU:1 before, /device:TPU:80 now
where the time goes in v1:
time: 191 us; the launch traced here: 190 us
  waiting for transfers between devices  76.4 us (40%)
  matrix products  44 us (23%)
  starting transfers between devices  38.8 us (20%)
  local copies, waits for them, and re-layouts  19.1 us (10%)
  other arithmetic  10.4 us (5%)
    ppermute x8, waiting for transfers between devices, shifted(): return lax.ppermute(value, axis, pairs)  45.4 us
    ppermute x8, starting transfers between devices, shifted(): return lax.ppermute(value, axis, pairs)  27.3 us
    sub x4, matrix products, head_grads(): weights = jnp.exp(masked - highest)  20.6 us
    ppermute x2, waiting for transfers between devices, body(): w1 = ppermute(summed, 'section', frame_out)  19.4 us
    unnamed x55, local copies, waits for them, and re-layouts  15.1 us
    convert_element_type x4, other arithmetic, head_grads(): probs_b = probs.astype(jnp.bfloat16)  8.43 us
    all_to_all x1, waiting for transfers between devices, body(): lax.all_to_all(shared_kv, 'tp', split_axis=2, concat_axis=1, tiled=True)  5.94 us
    dot_general x4, matrix products, head_grads(): jnp.einsum('rgd,ed->gre', grad_block, values_head, preferred_element_type...  5.86 us
  transfers between devices with their start and end apart: 12, of which 9 were waited for; matrix products, arithmetic and copies ran while one was open for 8% of the time, Pallas kernels for 0%

profile of v1, /device:TPU:80, one launch (start us, length us, event | category | flops | bytes accessed | tf_op | source)
XLA Modules:
  0.0 189.9 jit_solution(5957801366178075595)
XLA Ops:
  3.1 3.4 %all-to-all-start = ((bf16[4,2,16384]{2,1,0:T(2,128)(2,1)}), bf16[4,2,16384]{2,1,0:T(2,128)(2,1)S(1)}, u32[]{:S(2)}, u32[]{:S(2)}) async-start(bf16[4,2,16384]{2,1,0:T(2,128)(2,1)} %reshape.105), calls=%async_computation | async-start | bytes 524288 | tf_op jit(solution)/shard_map/all_to_all | solution.py:48
  6.5 5.9 %all-to-all-done = bf16[4,2,16384]{2,1,0:T(2,128)(2,1)S(1)} async-done(((bf16[4,2,16384]{2,1,0:T(2,128)(2,1)}), bf16[4,2,16384]{2,1,0:T(2,128)(2,1)S(1)}, u32[]{:S(2)}, u32[]{:S(2)}) %all-to-all-start) | async-done | bytes 262176 | tf_op jit(solution)/shard_map/all_to_all | solution.py:48
  13.9 6.4 %collective-permute-start = (bf16[2,256,256]{2,1,0:T(8,128)(2,1)}, bf16[2,256,256]{2,1,0:T(8,128)(2,1)}, u32[]{:S(2)}, u32[]{:S(2)}) collective-permute-start(bf16[2,256,256]{2,1,0:T(8,128)(2,1)} %bitcast.2), channel_id=1, source_target_pairs={{0,16},{4,20},{8,24},{12,28},{16,32},{20,36},{24,40},{28,44},{32,4... | collective-permute-start | bytes 786440 | tf_op jit(solution)/shard_map/ppermute | solution.py:17
  21.9 2.9 %collective-permute-start.2 = (bf16[2,256,256]{2,1,0:T(8,128)(2,1)}, bf16[2,256,256]{2,1,0:T(8,128)(2,1)}, u32[]{:S(2)}, u32[]{:S(2)}) collective-permute-start(bf16[2,256,256]{2,1,0:T(8,128)(2,1)} %bitcast.2), channel_id=1, source_target_pairs={{0,8},{4,12},{8,16},{12,20},{16,24},{20,28},{24,32},{28,36},{32,40... | collective-permute-start | bytes 786440 | tf_op jit(solution)/shard_map/ppermute | solution.py:17
  24.8 3.2 %collective-permute-start.1 = (bf16[2,256,256]{2,1,0:T(8,128)(2,1)}, bf16[2,256,256]{2,1,0:T(8,128)(2,1)}, u32[]{:S(2)}, u32[]{:S(2)}) collective-permute-start(bf16[2,256,256]{2,1,0:T(8,128)(2,1)} %bitcast.2), channel_id=1, source_target_pairs={{0,12},{4,16},{8,20},{12,24},{16,28},{20,32},{24,36},{28,40},{32,4... | collective-permute-start | bytes 786440 | tf_op jit(solution)/shard_map/ppermute | solution.py:17
  28.1 1.5 copy.145
  33.1 5.3 %collective-permute-start.3 = (bf16[2,256,256]{2,1,0:T(8,128)(2,1)}, bf16[2,256,256]{2,1,0:T(8,128)(2,1)S(1)}, u32[]{:S(2)}, u32[]{:S(2)}) collective-permute-start(bf16[2,256,256]{2,1,0:T(8,128)(2,1)} %bitcast.2), channel_id=1, source_target_pairs={{0,4},{4,8},{8,12},{12,16},{16,20},{20,24},{24,28},{28,32},{32,36}... | collective-permute-start | bytes 786440 | tf_op jit(solution)/shard_map/ppermute | solution.py:17
  39.4 10.3 %collective-permute-done.1 = bf16[2,256,256]{2,1,0:T(8,128)(2,1)} collective-permute-done((bf16[2,256,256]{2,1,0:T(8,128)(2,1)}, bf16[2,256,256]{2,1,0:T(8,128)(2,1)}, u32[]{:S(2)}, u32[]{:S(2)}) %collective-permute-start.1) | collective-permute-done | bytes 262176 | tf_op jit(solution)/shard_map/ppermute | solution.py:17
  51.6 2.3 %collective-permute-done.3 = bf16[2,256,256]{2,1,0:T(8,128)(2,1)S(1)} collective-permute-done((bf16[2,256,256]{2,1,0:T(8,128)(2,1)}, bf16[2,256,256]{2,1,0:T(8,128)(2,1)S(1)}, u32[]{:S(2)}, u32[]{:S(2)}) %collective-permute-start.3) | collective-permute-done | bytes 262176 | tf_op jit(solution)/shard_map/ppermute | solution.py:17
  54.9 5.3 %exponential_reduce_fusion.3 = (f32[4,256]{1,0:T(4,128)S(1)}, f32[4,256,1280]{1,2,0:T(8,128)}) fusion(pred[256,1280]{0,1:T(8,128)(4,1)} %fusion.28, bf16[256,16,128]{0,2,1:T(8,128)(2,1)S(1)} %bitcast.227, bf16[2,1280,256]{2,1,0:T(8,128)(2,1)S(1)} %constant_dynamic-update-slice_fusion), kind=kOutput, calls=%fused_computation.31 | convolution fusion | flops 340788480 | bytes 6164480 | tf_op jit(solution)/shard_map/sub | solution.py:27
  60.2 5.1 %exponential_reduce_fusion.1 = (f32[4,256]{1,0:T(4,128)S(1)}, f32[4,256,1280]{1,2,0:T(8,128)}) fusion(pred[256,1280]{0,1:T(8,128)(4,1)} %fusion.28, bf16[256,16,128]{0,2,1:T(8,128)(2,1)S(1)} %bitcast.228, bf16[2,1280,256]{2,1,0:T(8,128)(2,1)S(1)} %constant_dynamic-update-slice_fusion), kind=kOutput, calls=%fused_computation.27 | convolution fusion | flops 340788480 | bytes 6164480 | tf_op jit(solution)/shard_map/sub | solution.py:27
  65.3 5.1 %exponential_reduce_fusion.2 = (f32[4,256]{1,0:T(4,128)S(1)}, f32[4,256,1280]{1,2,0:T(8,128)}) fusion(pred[256,1280]{0,1:T(8,128)(4,1)} %fusion.28, bf16[256,16,128]{0,2,1:T(8,128)(2,1)S(1)} %bitcast.229, bf16[2,1280,256]{2,1,0:T(8,128)(2,1)S(1)} %constant_dynamic-update-slice_fusion), kind=kOutput, calls=%fused_computation.29 | convolution fusion | flops 340788480 | bytes 6164480 | tf_op jit(solution)/shard_map/sub | solution.py:27
  70.4 5.1 %exponential_reduce_fusion = (f32[4,256]{1,0:T(4,128)S(1)}, f32[4,256,1280]{1,2,0:T(8,128)}) fusion(pred[256,1280]{0,1:T(8,128)(4,1)} %fusion.28, bf16[256,16,128]{0,2,1:T(8,128)(2,1)S(1)} %bitcast.230, bf16[2,1280,256]{2,1,0:T(8,128)(2,1)S(1)} %constant_dynamic-update-slice_fusion), kind=kOutput, calls=%fused_computation.25 | convolution fusion | flops 340788480 | bytes 6164480 | tf_op jit(solution)/shard_map/sub | solution.py:27
  75.5 4.0 %fusion.23 = bf16[4,256,1280]{1,2,0:T(8,128)(2,1)S(1)} fusion(f32[4,256]{1,0:T(4,128)S(1)} %get-tuple-element.24, f32[4,256,1280]{1,2,0:T(8,128)} %get-tuple-element.25), kind=kLoop, calls=%fused_computation.50 | loop fusion | flops 2621440 | bytes 7868416 | tf_op jit(solution)/shard_map/convert_element_type | solution.py:29
  84.2 1.6 fusion.25
  90.6 1.4 fusion.24
  100.9 2.5 %fusion.9 = bf16[4,256,1280]{1,2,0:T(8,128)(2,1)S(1)} fusion(f32[4,256]{1,0:T(4,128)S(1)} %bitcast.240, f32[4,256]{1,0:T(4,128)S(1)} %get-tuple-element.18, f32[4,256,1280]{1,2,0:T(8,128)S(1)} %bitcast.220, bf16[2,1280,256]{2,1,0:T(8,128)(2,1)S(1)} %copy-done.2, bf16[256,16,128]{0,2,1:T(8,128)(2,1)} %bitcast.218), kind=kOutput, calls=%fused_computation.10 | convolution fusion | flops 340787200 | bytes 8462336 | tf_op jit(solution)/shard_map/rgd,ed->gre/dot_general | solution.py:32
  105.8 1.9 %collective-permute-start.4 = (bf16[2,256,256]{1,2,0:T(8,128)(2,1)S(1)}, bf16[2,256,256]{1,2,0:T(8,128)(2,1)S(1)}, u32[]{:S(2)}, u32[]{:S(2)}) collective-permute-start(bf16[2,256,256]{1,2,0:T(8,128)(2,1)S(1)} %get-tuple-element.10), channel_id=1, source_target_pairs={{16,0},{20,4},{24,8},{28,12},{32,16},{36,20},{40,24},{44,28},{48,3... | collective-permute-start | bytes 786440 | tf_op jit(solution)/shard_map/ppermute | solution.py:17
  107.8 3.8 %collective-permute-start.7 = (bf16[2,256,256]{1,2,0:T(8,128)(2,1)S(1)}, bf16[2,256,256]{1,2,0:T(8,128)(2,1)S(1)}, u32[]{:S(2)}, u32[]{:S(2)}) collective-permute-start(bf16[2,256,256]{1,2,0:T(8,128)(2,1)S(1)} %get-tuple-element.11), channel_id=1, source_target_pairs={{4,0},{8,4},{12,8},{16,12},{20,16},{24,20},{28,24},{32,28},{36,32}... | collective-permute-start | bytes 786440 | tf_op jit(solution)/shard_map/ppermute | solution.py:17
  111.5 1.9 %collective-permute-start.6 = (bf16[2,256,256]{1,2,0:T(8,128)(2,1)S(1)}, bf16[2,256,256]{1,2,0:T(8,128)(2,1)S(1)}, u32[]{:S(2)}, u32[]{:S(2)}) collective-permute-start(bf16[2,256,256]{1,2,0:T(8,128)(2,1)S(1)} %get-tuple-element.12), channel_id=1, source_target_pairs={{8,0},{12,4},{16,8},{20,12},{24,16},{28,20},{32,24},{36,28},{40,32... | collective-permute-start | bytes 786440 | tf_op jit(solution)/shard_map/ppermute | solution.py:17
  113.5 1.9 %collective-permute-start.5 = (bf16[2,256,256]{1,2,0:T(8,128)(2,1)S(1)}, bf16[2,256,256]{1,2,0:T(8,128)(2,1)S(1)}, u32[]{:S(2)}, u32[]{:S(2)}) collective-permute-start(bf16[2,256,256]{1,2,0:T(8,128)(2,1)S(1)} %get-tuple-element.13), channel_id=1, source_target_pairs={{12,0},{16,4},{20,8},{24,12},{28,16},{32,20},{36,24},{40,28},{44,3... | collective-permute-start | bytes 786440 | tf_op jit(solution)/shard_map/ppermute | solution.py:17
  115.4 8.5 %collective-permute-done.4 = bf16[2,256,256]{1,2,0:T(8,128)(2,1)S(1)} collective-permute-done((bf16[2,256,256]{1,2,0:T(8,128)(2,1)S(1)}, bf16[2,256,256]{1,2,0:T(8,128)(2,1)S(1)}, u32[]{:S(2)}, u32[]{:S(2)}) %collective-permute-start.4) | collective-permute-done | bytes 262176 | tf_op jit(solution)/shard_map/ppermute | solution.py:17
  123.9 7.0 %collective-permute-done.7 = bf16[2,256,256]{1,2,0:T(8,128)(2,1)S(1)} collective-permute-done((bf16[2,256,256]{1,2,0:T(8,128)(2,1)S(1)}, bf16[2,256,256]{1,2,0:T(8,128)(2,1)S(1)}, u32[]{:S(2)}, u32[]{:S(2)}) %collective-permute-start.7) | collective-permute-done | bytes 262176 | tf_op jit(solution)/shard_map/ppermute | solution.py:17
  131.0 17.3 %collective-permute-done.5 = bf16[2,256,256]{1,2,0:T(8,128)(2,1)S(1)} collective-permute-done((bf16[2,256,256]{1,2,0:T(8,128)(2,1)S(1)}, bf16[2,256,256]{1,2,0:T(8,128)(2,1)S(1)}, u32[]{:S(2)}, u32[]{:S(2)}) %collective-permute-start.5) | collective-permute-done | bytes 262176 | tf_op jit(solution)/shard_map/ppermute | solution.py:17
  148.4 1.6 collective-permute-start.8
  150.5 11.1 %collective-permute-done.8 = f32[2,256,256]{1,2,0:T(8,128)S(1)} collective-permute-done((f32[2,256,256]{1,2,0:T(8,128)S(1)}, f32[2,256,256]{1,2,0:T(8,128)S(1)}, u32[]{:S(2)}, u32[]{:S(2)}) %collective-permute-start.8) | collective-permute-done | bytes 524320 | tf_op jit(solution)/shard_map/ppermute | solution.py:102
  161.7 3.1 %collective-permute-start.9 = (f32[2,256,256]{1,2,0:T(8,128)S(1)}, f32[2,256,256]{1,2,0:T(8,128)S(1)}, u32[]{:S(2)}, u32[]{:S(2)}) collective-permute-start(f32[2,256,256]{1,2,0:T(8,128)S(1)} %add.66), channel_id=1, source_target_pairs={{0,128},{64,192},{128,0},{192,64},{1,129},{65,193},{129,1},{193,65... | collective-permute-start | bytes 1572872 | tf_op jit(solution)/shard_map/ppermute | solution.py:102
  167.4 8.3 %collective-permute-done.9 = f32[2,256,256]{1,2,0:T(8,128)S(1)} collective-permute-done((f32[2,256,256]{1,2,0:T(8,128)S(1)}, f32[2,256,256]{1,2,0:T(8,128)S(1)}, u32[]{:S(2)}, u32[]{:S(2)}) %collective-permute-start.9) | collective-permute-done | bytes 524320 | tf_op jit(solution)/shard_map/ppermute | solution.py:102
  176.7 3.5 %all-to-all-start.1 = ((f32[2,256,256]{2,0,1:T(2,128)}), f32[2,256,256]{2,0,1:T(2,128)S(1)}, u32[]{:S(2)}, u32[]{:S(2)}) async-start(f32[2,256,256]{2,0,1:T(2,128)} %copy.191), calls=%async_computation.1 | async-start | bytes 1048576 | tf_op jit(solution)/shard_map/all_to_all | solution.py:104
  180.2 1.6 fusion.41
  182.0 1.4 copy.194
  183.4 5.6 %all-to-all-done.1 = f32[2,256,256]{2,0,1:T(2,128)S(1)} async-done(((f32[2,256,256]{2,0,1:T(2,128)}), f32[2,256,256]{2,0,1:T(2,128)S(1)}, u32[]{:S(2)}, u32[]{:S(2)}) %all-to-all-start.1) | async-done | bytes 524320 | tf_op jit(solution)/shard_map/all_to_all | solution.py:104
  (95 shorter events, 38.9 us)
Async XLA Ops:
  0.6 20.7 %copy-start.9 = (bf16[1,256,2048]{2,1,0:T(8,128)(2,1)S(1)}, bf16[1,256,2048]{2,1,0:T(8,128)(2,1)}, u32[]{:S(2)}) copy-start(bf16[1,256,2048]{2,1,0:T(8,128)(2,1)} %param.4) | copy-start | bytes 3145732
  3.1 9.4 %all-to-all-start = ((bf16[4,2,16384]{2,1,0:T(2,128)(2,1)}), bf16[4,2,16384]{2,1,0:T(2,128)(2,1)S(1)}, u32[]{:S(2)}, u32[]{:S(2)}) async-start(bf16[4,2,16384]{2,1,0:T(2,128)(2,1)} %reshape.105), calls=%async_computation | async-start | bytes 524288 | tf_op jit(solution)/shard_map/all_to_all | solution.py:48
  13.9 24.5 %collective-permute-start = (bf16[2,256,256]{2,1,0:T(8,128)(2,1)}, bf16[2,256,256]{2,1,0:T(8,128)(2,1)}, u32[]{:S(2)}, u32[]{:S(2)}) collective-permute-start(bf16[2,256,256]{2,1,0:T(8,128)(2,1)} %bitcast.2), channel_id=1, source_target_pairs={{0,16},{4,20},{8,24},{12,28},{16,32},{20,36},{24,40},{28,44},{32,4... | collective-permute-start | bytes 786440 | tf_op jit(solution)/shard_map/ppermute | solution.py:17
  21.9 77.7 %copy-start = (bf16[1,256,2048]{1,2,0:T(8,128)(2,1)}, bf16[1,256,2048]{1,2,0:T(8,128)(2,1)S(1)}, u32[]{:S(2)}) copy-start(bf16[1,256,2048]{1,2,0:T(8,128)(2,1)S(1)} %copy.147) | copy-start | bytes 3145732
  21.9 28.7 %collective-permute-start.2 = (bf16[2,256,256]{2,1,0:T(8,128)(2,1)}, bf16[2,256,256]{2,1,0:T(8,128)(2,1)}, u32[]{:S(2)}, u32[]{:S(2)}) collective-permute-start(bf16[2,256,256]{2,1,0:T(8,128)(2,1)} %bitcast.2), channel_id=1, source_target_pairs={{0,8},{4,12},{8,16},{12,20},{16,24},{20,28},{24,32},{28,36},{32,40... | collective-permute-start | bytes 786440 | tf_op jit(solution)/shard_map/ppermute | solution.py:17
  24.8 24.8 %collective-permute-start.1 = (bf16[2,256,256]{2,1,0:T(8,128)(2,1)}, bf16[2,256,256]{2,1,0:T(8,128)(2,1)}, u32[]{:S(2)}, u32[]{:S(2)}) collective-permute-start(bf16[2,256,256]{2,1,0:T(8,128)(2,1)} %bitcast.2), channel_id=1, source_target_pairs={{0,12},{4,16},{8,20},{12,24},{16,28},{20,32},{24,36},{28,40},{32,4... | collective-permute-start | bytes 786440 | tf_op jit(solution)/shard_map/ppermute | solution.py:17
  29.6 59.7 %copy-start.3 = (bf16[1,256,2048]{1,2,0:T(8,128)(2,1)}, bf16[1,256,2048]{1,2,0:T(8,128)(2,1)S(1)}, u32[]{:S(2)}) copy-start(bf16[1,256,2048]{1,2,0:T(8,128)(2,1)S(1)} %copy.145) | copy-start | bytes 3145732
  33.1 20.8 %collective-permute-start.3 = (bf16[2,256,256]{2,1,0:T(8,128)(2,1)}, bf16[2,256,256]{2,1,0:T(8,128)(2,1)S(1)}, u32[]{:S(2)}, u32[]{:S(2)}) collective-permute-start(bf16[2,256,256]{2,1,0:T(8,128)(2,1)} %bitcast.2), channel_id=1, source_target_pairs={{0,4},{4,8},{8,12},{12,16},{16,20},{20,24},{24,28},{28,32},{32,36}... | collective-permute-start | bytes 786440 | tf_op jit(solution)/shard_map/ppermute | solution.py:17
  54.9 43.4 %copy-start.1 = (bf16[2,1280,256]{2,1,0:T(8,128)(2,1)}, bf16[2,1280,256]{2,1,0:T(8,128)(2,1)S(1)}, u32[]{:S(2)}) copy-start(bf16[2,1280,256]{2,1,0:T(8,128)(2,1)S(1)} %constant_dynamic-update-slice_fusion) | copy-start | bytes 3932164
  75.5 6.3 %slice-start.6 = ((s8[5242880]{0:T(1024)(128)(4,1)}), s8[4194304]{0:T(1024)(128)(4,1)S(1)}, s32[]{:S(2)}) async-start(s8[5242880]{0:T(1024)(128)(4,1)} %bitcast.225), calls=%async_computation.8 | async-start | bytes 8388608
  79.4 1.0 copy-start.8
  79.5 2.3 %slice-start.7 = ((s8[5242880]{0:T(1024)(128)(4,1)}), s8[1048576]{0:T(1024)(128)(4,1)S(1)}, s32[]{:S(2)}) async-start(s8[5242880]{0:T(1024)(128)(4,1)} %bitcast.225), calls=%async_computation.9 | async-start | bytes 2097152
  81.7 2.2 %slice-start.4 = ((s8[5242880]{0:T(1024)(128)(4,1)}), s8[4194304]{0:T(1024)(128)(4,1)S(1)}, s32[]{:S(2)}) async-start(s8[5242880]{0:T(1024)(128)(4,1)} %bitcast.223), calls=%async_computation.6 | async-start | bytes 8388608
  81.8 2.5 %slice-start.5 = ((s8[5242880]{0:T(1024)(128)(4,1)}), s8[1048576]{0:T(1024)(128)(4,1)S(1)}, s32[]{:S(2)}) async-start(s8[5242880]{0:T(1024)(128)(4,1)} %bitcast.223), calls=%async_computation.7 | async-start | bytes 2097152
  85.9 1.0 copy-start.7
  88.2 2.2 %slice-start.2 = ((s8[5242880]{0:T(1024)(128)(4,1)}), s8[4194304]{0:T(1024)(128)(4,1)S(1)}, s32[]{:S(2)}) async-start(s8[5242880]{0:T(1024)(128)(4,1)} %bitcast.221), calls=%async_computation.4 | async-start | bytes 8388608
  88.2 2.5 %slice-start.3 = ((s8[5242880]{0:T(1024)(128)(4,1)}), s8[1048576]{0:T(1024)(128)(4,1)S(1)}, s32[]{:S(2)}) async-start(s8[5242880]{0:T(1024)(128)(4,1)} %bitcast.221), calls=%async_computation.5 | async-start | bytes 2097152
  90.6 1.4 copy-start.6
  94.3 2.2 %slice-start = ((s8[5242880]{0:T(1024)(128)(4,1)}), s8[4194304]{0:T(1024)(128)(4,1)S(1)}, s32[]{:S(2)}) async-start(s8[5242880]{0:T(1024)(128)(4,1)} %bitcast.219), calls=%async_computation.2 | async-start | bytes 8388608
  94.4 2.5 %slice-start.1 = ((s8[5242880]{0:T(1024)(128)(4,1)}), s8[1048576]{0:T(1024)(128)(4,1)S(1)}, s32[]{:S(2)}) async-start(s8[5242880]{0:T(1024)(128)(4,1)} %bitcast.219), calls=%async_computation.3 | async-start | bytes 2097152
  96.8 1.4 copy-start.5
  99.6 1.3 copy-start.2
  100.9 2.5 %copy-start.4 = (bf16[1,256,2048]{1,2,0:T(8,128)(2,1)S(1)}, bf16[1,256,2048]{1,2,0:T(8,128)(2,1)}, u32[]{:S(2)}) copy-start(bf16[1,256,2048]{1,2,0:T(8,128)(2,1)} %copy-done.3) | copy-start | bytes 3145732
  105.8 18.1 %collective-permute-start.4 = (bf16[2,256,256]{1,2,0:T(8,128)(2,1)S(1)}, bf16[2,256,256]{1,2,0:T(8,128)(2,1)S(1)}, u32[]{:S(2)}, u32[]{:S(2)}) collective-permute-start(bf16[2,256,256]{1,2,0:T(8,128)(2,1)S(1)} %get-tuple-element.10), channel_id=1, source_target_pairs={{16,0},{20,4},{24,8},{28,12},{32,16},{36,20},{40,24},{44,28},{48,3... | collective-permute-start | bytes 786440 | tf_op jit(solution)/shard_map/ppermute | solution.py:17
  107.8 23.2 %collective-permute-start.7 = (bf16[2,256,256]{1,2,0:T(8,128)(2,1)S(1)}, bf16[2,256,256]{1,2,0:T(8,128)(2,1)S(1)}, u32[]{:S(2)}, u32[]{:S(2)}) collective-permute-start(bf16[2,256,256]{1,2,0:T(8,128)(2,1)S(1)} %get-tuple-element.11), channel_id=1, source_target_pairs={{4,0},{8,4},{12,8},{16,12},{20,16},{24,20},{28,24},{32,28},{36,32}... | collective-permute-start | bytes 786440 | tf_op jit(solution)/shard_map/ppermute | solution.py:17
  111.5 19.4 %collective-permute-start.6 = (bf16[2,256,256]{1,2,0:T(8,128)(2,1)S(1)}, bf16[2,256,256]{1,2,0:T(8,128)(2,1)S(1)}, u32[]{:S(2)}, u32[]{:S(2)}) collective-permute-start(bf16[2,256,256]{1,2,0:T(8,128)(2,1)S(1)} %get-tuple-element.12), channel_id=1, source_target_pairs={{8,0},{12,4},{16,8},{20,12},{24,16},{28,20},{32,24},{36,28},{40,32... | collective-permute-start | bytes 786440 | tf_op jit(solution)/shard_map/ppermute | solution.py:17
  113.5 34.8 %collective-permute-start.5 = (bf16[2,256,256]{1,2,0:T(8,128)(2,1)S(1)}, bf16[2,256,256]{1,2,0:T(8,128)(2,1)S(1)}, u32[]{:S(2)}, u32[]{:S(2)}) collective-permute-start(bf16[2,256,256]{1,2,0:T(8,128)(2,1)S(1)} %get-tuple-element.13), channel_id=1, source_target_pairs={{12,0},{16,4},{20,8},{24,12},{28,16},{32,20},{36,24},{40,28},{44,3... | collective-permute-start | bytes 786440 | tf_op jit(solution)/shard_map/ppermute | solution.py:17
  148.4 13.3 %collective-permute-start.8 = (f32[2,256,256]{1,2,0:T(8,128)S(1)}, f32[2,256,256]{1,2,0:T(8,128)S(1)}, u32[]{:S(2)}, u32[]{:S(2)}) collective-permute-start(f32[2,256,256]{1,2,0:T(8,128)S(1)} %fusion.49), channel_id=1, source_target_pairs={{0,64},{64,0},{128,192},{192,128},{1,65},{65,1},{129,193},{193,129... | collective-permute-start | bytes 1572872 | tf_op jit(solution)/shard_map/ppermute | solution.py:102
  161.7 13.9 %collective-permute-start.9 = (f32[2,256,256]{1,2,0:T(8,128)S(1)}, f32[2,256,256]{1,2,0:T(8,128)S(1)}, u32[]{:S(2)}, u32[]{:S(2)}) collective-permute-start(f32[2,256,256]{1,2,0:T(8,128)S(1)} %add.66), channel_id=1, source_target_pairs={{0,128},{64,192},{128,0},{192,64},{1,129},{65,193},{129,1},{193,65... | collective-permute-start | bytes 1572872 | tf_op jit(solution)/shard_map/ppermute | solution.py:102
  176.7 12.3 %all-to-all-start.1 = ((f32[2,256,256]{2,0,1:T(2,128)}), f32[2,256,256]{2,0,1:T(2,128)S(1)}, u32[]{:S(2)}, u32[]{:S(2)}) async-start(f32[2,256,256]{2,0,1:T(2,128)} %copy.191), calls=%async_computation.1 | async-start | bytes 1048576 | tf_op jit(solution)/shard_map/all_to_all | solution.py:104
  180.2 1.6 copy-start.10
  180.2 1.6 copy-start.11
